TPU v7x, 256 devices: a whole 4x4x8 slice. The times are simulated.
256 devices in a mesh: seq: 64 (over x, z, core), head: 4 (over y).
Axes of the slice: x: 4, y: 4, z: 8, core: 2. Of those that a mesh axis runs over, the one named last changes fastest.
Arguments:
- queries: bfloat16 [65536, 2048], P('seq', 'head'), may hold values from -48 to 48
- keys: bfloat16 [65536, 2048], P('seq', 'head'), may hold values from -48 to 48
- values: bfloat16 [65536, 2048], P('seq', 'head'), may hold values from -6 to 6
- memory_keys: bfloat16 [65536, 2048], P('seq', 'head'), may hold values from -48 to 48
- memory_values: bfloat16 [65536, 2048], P('seq', 'head'), may hold values from -6 to 6
- block_ids: int32 [512, 4], P('seq'), may hold values from 0 to 1023, as said below
- gate_bias: float32 [16], P('head'), may hold values from -2 to 2
- out_weight: bfloat16 [2048, 2048], P('head'), may hold values from -0.5 to 0.5
Outputs:
- layer_out: bfloat16 [65536, 2048], P(('seq', 'head'))
Inputs may be any that keep to these rules, and one draw needn't show every extreme that they name: `block_ids`: block b belongs to owner b // 16. Among the 8 x 4 ids of one device's rows no id repeats; exactly 2 of them name blocks of owner 64 - 1, block 1023 always among them, and no other owner is named more than 1 times.
All inputs are finite; a program needn't handle non-finite values.
Results may differ from a plain program's by a relative error of at most 0.013.
Values may be sent and summed in bfloat16 or wider, within the bound.
No kernel may reach another device: no remote copies, remote signals or barrier semaphores. Data moves between devices by JAX's collectives and lax.ppermute only.
A program may use at most 192 MiB of HBM per device.

v0:
```python
import math
import jax
import jax.numpy as jnp
from jax import lax
from jax.sharding import PartitionSpec as P

HDIM = 128
WINDOW = 1024
QBLK = 128
MROWS = 64
TOPM = 4
NEG_FILL = -1e30


def passed_along(value, axis, steps):
    count = lax.axis_size(axis)
    leading, last = (max(0, -steps), min(count, count - steps))
    return lax.ppermute(value, axis, [(source, source + steps) for source in range(leading, last)])


def masked_softmax(scores, allowed):
    row_max = jnp.max(jnp.where(allowed, scores, NEG_FILL), axis=-1, keepdims=True)
    weights = jnp.where(allowed, jnp.exp(scores - row_max), 0.0)
    return (weights / jnp.sum(weights, axis=-1, keepdims=True)).astype(jnp.bfloat16)


def window_attention(queries, ext_keys, ext_values, first_row):
    tok_rows, features = queries.shape
    heads_here = features // HDIM
    tile_rows = math.gcd(tok_rows, 512)
    key_span = tile_rows + WINDOW
    score_scale = 1.0 / math.sqrt(HDIM)

    def per_tile(step_index):
        row_start = step_index * tile_rows
        query_tile = lax.dynamic_slice_in_dim(queries, row_start, tile_rows, 0).reshape(
            tile_rows, heads_here, HDIM
        )
        key_tile = lax.dynamic_slice_in_dim(ext_keys, row_start, key_span, 0).reshape(
            key_span, heads_here, HDIM
        )
        value_tile = lax.dynamic_slice_in_dim(ext_values, row_start, key_span, 0).reshape(
            key_span, heads_here, HDIM
        )
        scores = (
            jnp.einsum("qhd,khd->hqk", query_tile, key_tile, preferred_element_type=jnp.float32)
            * score_scale
        )
        query_pos = first_row + row_start + jnp.arange(tile_rows, dtype=jnp.int32)
        key_pos = first_row + row_start - WINDOW + jnp.arange(key_span, dtype=jnp.int32)
        allowed = (
            (key_pos[None, :] <= query_pos[:, None])
            & (key_pos[None, :] > query_pos[:, None] - WINDOW)
            & (key_pos[None, :] >= 0)
        )
        attend_weights = masked_softmax(scores, allowed[None])
        return jnp.einsum(
            "hqk,khd->qhd", attend_weights, value_tile, preferred_element_type=jnp.float32
        )

    return lax.map(per_tile, jnp.arange(tok_rows // tile_rows, dtype=jnp.int32)).reshape(
        tok_rows, heads_here, HDIM
    )


def memory_attention(queries, fetched):
    tok_rows, features = queries.shape
    heads_here = features // HDIM
    block_count = tok_rows // QBLK
    score_scale = 1.0 / math.sqrt(HDIM)
    query_blocks = queries.reshape(block_count, QBLK, heads_here, HDIM)
    key_blocks = fetched[:, 0].reshape(block_count, TOPM * MROWS, heads_here, HDIM)
    value_blocks = fetched[:, 1].reshape(block_count, TOPM * MROWS, heads_here, HDIM)
    scores = (
        jnp.einsum("bqhd,bkhd->bhqk", query_blocks, key_blocks, preferred_element_type=jnp.float32)
        * score_scale
    )
    attend_weights = masked_softmax(scores, jnp.ones(scores.shape, dtype=bool))
    remote = jnp.einsum(
        "bhqk,bkhd->bqhd", attend_weights, value_blocks, preferred_element_type=jnp.float32
    )
    return remote.reshape(tok_rows, heads_here, HDIM)


def build_table(slot_index, offset, in_use, total_slots):
    matches = (jnp.arange(total_slots, dtype=jnp.int32)[:, None] == slot_index[None, :]) & in_use[
        None, :
    ]
    return jnp.sum(jnp.where(matches, offset[None, :] + 1, 0), axis=1) - 1


def on_device(queries, keys, values, memory_keys, memory_values, block_ids, gate_bias, out_weight):
    tok_rows, features = queries.shape
    owners = lax.axis_size("seq")
    groups = lax.axis_size("head")
    seq_index = lax.axis_index("seq")
    first_row = seq_index * tok_rows
    full_weight = lax.all_gather(out_weight, "head", axis=0, tiled=True)
    request_count = block_ids.shape[0] * block_ids.shape[1]
    wanted = block_ids.reshape(request_count)
    mem_dev = memory_keys.shape[0] // MROWS
    last_block = owners * mem_dev - 1
    owner_index = wanted // mem_dev
    offset = wanted % mem_dev
    is_last = wanted == last_block
    memory_store = jnp.stack(
        (
            memory_keys.reshape(mem_dev, MROWS, features),
            memory_values.reshape(mem_dev, MROWS, features),
        ),
        axis=1,
    )
    edge_rows = jnp.stack((keys, values))
    before = passed_along(edge_rows, "seq", 1)
    shared = lax.psum(
        jnp.where(
            seq_index == owners - 1, memory_store[mem_dev - 1], jnp.zeros_like(memory_store[0])
        ),
        "seq",
    )
    every_id = lax.all_gather(block_ids, "seq", axis=0, tiled=True).reshape(owners, request_count)
    mine = (every_id // mem_dev == seq_index) & (every_id != last_block)
    asked_for = jnp.sum(jnp.where(mine, every_id % mem_dev + 1, 0), axis=1) - 1
    outgoing = memory_store[jnp.maximum(asked_for, 0)]
    before, outgoing, shared = lax.optimization_barrier((before, outgoing, shared))
    returned = lax.all_to_all(outgoing, "seq", split_axis=0, concat_axis=0, tiled=True)
    local_part = window_attention(
        queries, jnp.concatenate([before[0], keys]), jnp.concatenate([before[1], values]), first_row
    )
    fetched = jnp.where(is_last[:, None, None, None], shared[None], returned[owner_index])
    remote = memory_attention(queries, fetched)
    mixing = jax.nn.sigmoid(gate_bias)[None, :, None]
    attended = (
        (mixing * remote + (1.0 - mixing) * local_part)
        .reshape(tok_rows, features)
        .astype(jnp.bfloat16)
    )
    out_rows = tok_rows // groups
    gathered = lax.all_to_all(
        attended.reshape(groups, out_rows, features),
        "head",
        split_axis=0,
        concat_axis=0,
        tiled=True,
    )
    partials = jnp.einsum(
        "gqf,gfn->gqn",
        gathered,
        full_weight.reshape(groups, features, full_weight.shape[1]),
        preferred_element_type=jnp.float32,
    ).astype(jnp.bfloat16)
    return jnp.sum(partials.astype(jnp.float32), axis=0).astype(jnp.bfloat16)


def solution(mesh):
    in_specs = (
        P("seq", "head"),
        P("seq", "head"),
        P("seq", "head"),
        P("seq", "head"),
        P("seq", "head"),
        P("seq", None),
        P("head"),
        P("head", None),
    )
    out_specs = P(("seq", "head"), None)
    return jax.shard_map(
        on_device, mesh=mesh, in_specs=in_specs, out_specs=out_specs, check_vma=False
    )
```

profile of v0, /device:TPU:1, one launch (start us, length us, event | category | flops | bytes accessed | tf_op | source)
XLA Modules:
  0.0 452.9 jit_solution(179319438945823830)
XLA Ops:
  11.2 5.0 %collective-permute-start = (bf16[2,1024,512]{1,2,0:T(8,128)(2,1)}, bf16[2,1024,512]{1,2,0:T(8,128)(2,1)}, u32[]{:S(2)}, u32[]{:S(2)}) collective-permute-start(bf16[2,1024,512]{1,2,0:T(8,128)(2,1)} %pad_maximum_fusion.1), channel_id=1, source_target_pairs={{0,4},{4,8},{8,12},{12,16},{16,20},{20,24},{24,28},{28,32},{32,36}... | collective-permute-start | bytes 6291464 | tf_op jit(solution)/shard_map/ppermute | solution.py:18
  17.8 62.6 %all-gather = s32[64,8,4]{1,2,0:T(4,128)S(1)} all-gather(s32[1,8,4]{1,2,0:T(4,128)S(1)} %bitcast.85), channel_id=1, replica_groups=mesh['seq'=64,'head'=4] {'seq'}, dimensions={0}, use_global_device_ids=true | all-gather | bytes 8320 | tf_op jit(solution)/shard_map/all_gather | solution.py:121
  82.5 5.5 %gather_fusion = bf16[64,2,64,512]{3,2,1,0:T(8,128)(2,1)} fusion(bf16[16,2,64,512]{3,2,1,0:T(8,128)(2,1)S(1)} %pad_maximum_fusion, s32[1024]{0:T(1024)S(1)} %pad_clamp_fusion.1), kind=kCustom, calls=%fused_computation | custom fusion | bytes 16777472 | tf_op jit(solution)/shard_map/gather | solution.py:124
  88.0 108.2 %all-reduce.2.cloned.1.call-done = bf16[2,64,512]{2,1,0:T(8,128)(2,1)} async-done(((bf16[2,64,512]{2,1,0:T(8,128)(2,1)}), bf16[2,64,512]{2,1,0:T(8,128)(2,1)}) %all-reduce.2.cloned.1.call-update) | async-done | bytes 131088 | tf_op jit(solution)/shard_map/psum | solution.py:115
  196.2 6.7 %all-to-all-start = ((bf16[64,2,64,512]{3,2,1,0:T(8,128)(2,1)}), bf16[64,2,64,512]{3,2,1,0:T(8,128)(2,1)}, u32[]{:S(2)}, u32[]{:S(2)}) async-start(bf16[64,2,64,512]{3,2,1,0:T(8,128)(2,1)} %gather_fusion), calls=%async_computation | async-start | bytes 16777216 | tf_op jit(solution)/shard_map/all_to_all | solution.py:126
  209.4 60.5 %while.13 = (s32[]{:T(128)}, f32[2,512,4,128]{3,2,1,0:T(4,128)}, s32[2]{0:T(128)S(1)}, bf16[2048,512]{0,1:T(8,128)(2,1)S(1)}, s32[]{:T(128)}, /*index=5*/bf16[10...) while((s32[]{:T(128)}, f32[2,512,4,128]{3,2,1,0:T(4,128)}, ...), condition=%wide.region_8.9_spmd, body=%wide.region_5.8_spmd.sunk | while | flops 2444237824 | bytes 44080892 | solution.py:61
  211.5 3.3 constant_dynamic-slice_fusion.5
  216.9 11.6 %fusion.59 = (f32[4,512]{1,0:T(4,128)S(1)}, f32[4,512,1536]{2,1,0:T(8,128)}) fusion(pred[512,1536]{1,0:T(8,128)(4,1)S(1)} %and_and_fusion.2, bf16[512,4,128]{0,2,1:T(8,128)(2,1)} %bitcast.78, bf16[1536,4,128]{0,2,1:T(8,128)(2,1)} %bitcast.77), kind=kOutput, calls=%fused_computation.78.clone.1 | convolution fusion | flops 1629488640 | bytes 15474688 | tf_op jit(solution)/shard_map/while/body/eval_jaxpr/sub | solution.py:23
  228.5 8.5 %fusion.60 = f32[1,512,4,128]{1,3,2,0:T(8,128)} fusion(bf16[1536,4,128]{0,2,1:T(8,128)(2,1)} %bitcast.76, f32[4,512,1536]{2,1,0:T(8,128)} %get-tuple-element.234, f32[4,512]{1,0:T(4,128)S(1)} %get-tuple-element.235), kind=kOutput, calls=%fused_computation.14.clone.1 | convolution fusion | flops 811597824 | bytes 15212544 | tf_op jit(solution)/shard_map/while/body/eval_jaxpr/hqk,khd->qhd/dot_general | solution.py:57
  241.8 3.4 constant_dynamic-slice_fusion.5
  247.2 11.6 %fusion.59 = (f32[4,512]{1,0:T(4,128)S(1)}, f32[4,512,1536]{2,1,0:T(8,128)}) fusion(pred[512,1536]{1,0:T(8,128)(4,1)S(1)} %and_and_fusion.2, bf16[512,4,128]{0,2,1:T(8,128)(2,1)} %bitcast.78, bf16[1536,4,128]{0,2,1:T(8,128)(2,1)} %bitcast.77), kind=kOutput, calls=%fused_computation.78.clone.1 | convolution fusion | flops 1629488640 | bytes 15474688 | tf_op jit(solution)/shard_map/while/body/eval_jaxpr/sub | solution.py:23
  258.8 8.4 %fusion.60 = f32[1,512,4,128]{1,3,2,0:T(8,128)} fusion(bf16[1536,4,128]{0,2,1:T(8,128)(2,1)} %bitcast.76, f32[4,512,1536]{2,1,0:T(8,128)} %get-tuple-element.234, f32[4,512]{1,0:T(4,128)S(1)} %get-tuple-element.235), kind=kOutput, calls=%fused_computation.14.clone.1 | convolution fusion | flops 811597824 | bytes 15212544 | tf_op jit(solution)/shard_map/while/body/eval_jaxpr/hqk,khd->qhd/dot_general | solution.py:57
  269.9 3.1 reshape.263
  273.1 115.5 %all-to-all-done = bf16[64,2,64,512]{3,2,1,0:T(8,128)(2,1)} async-done(((bf16[64,2,64,512]{3,2,1,0:T(8,128)(2,1)}), bf16[64,2,64,512]{3,2,1,0:T(8,128)(2,1)}, u32[]{:S(2)}, u32[]{:S(2)}) %all-to-all-start) | async-done | bytes 8388640 | tf_op jit(solution)/shard_map/all_to_all | solution.py:126
  388.6 6.2 %gather_fusion.1 = bf16[32,2,64,512]{3,2,1,0:T(8,128)(2,1)} fusion(bf16[64,2,64,512]{3,2,1,0:T(8,128)(2,1)} %all-to-all-done, s32[1024]{0:T(1024)S(1)} %pad_clamp_fusion), kind=kCustom, calls=%fused_computation.1 | custom fusion | bytes 8388736 | tf_op jit(solution)/shard_map/gather | solution.py:130
  394.8 2.6 broadcast_select_fusion
  399.6 2.5 reshape_squeeze.7
  402.2 4.1 reshape_squeeze.6
  407.0 3.1 fusion.39
  412.9 3.2 reshape.262
  416.1 3.1 add_convert_fusion
  419.2 4.0 all-to-all-start.1
  423.2 15.3 %all-to-all-done.1 = bf16[4,256,512]{2,1,0:T(8,128)(2,1)S(1)} async-done(((bf16[4,256,512]{2,1,0:T(8,128)(2,1)}), bf16[4,256,512]{2,1,0:T(8,128)(2,1)S(1)}, u32[]{:S(2)}, u32[]{:S(2)}) %all-to-all-start.1) | async-done | bytes 1048608 | tf_op jit(solution)/shard_map/all_to_all | solution.py:139
  438.5 6.9 %convert_reduce_fusion = bf16[256,2048]{1,0:T(8,128)(2,1)} fusion(bf16[4,256,512]{2,1,0:T(8,128)(2,1)S(1)} %all-to-all-done.1, bf16[4,512,2048]{2,1,0:T(8,128)(2,1)} %bitcast.86), kind=kOutput, calls=%fused_computation.30 | convolution fusion | flops 2151153664 | bytes 10485760 | tf_op jit(solution)/shard_map/gqf,gfn->gqn/dot_general | solution.py:146
  (80 shorter events, 32.0 us)
Async XLA Ops:
  7.4 1.6 copy-start.7
  7.4 188.8 %all-reduce.2.cloned.1.call-start = ((), (), s32[]{:S(2)}) async-start(), calls=%async_computation.2 | async-start | bytes 262144 | tf_op jit(solution)/shard_map/psum | solution.py:115
  9.5 1.7 copy-start.1
  9.5 6.7 %copy-start.5 = (bf16[1024,512]{1,0:T(8,128)(2,1)S(1)}, bf16[1024,512]{1,0:T(8,128)(2,1)}, u32[]{:S(2)}) copy-start(bf16[1024,512]{1,0:T(8,128)(2,1)} %param.14) | copy-start | bytes 3145732
  11.2 6.6 %copy-start.9 = (s32[8,4]{0,1:T(4,128)S(1)}, s32[8,4]{0,1:T(4,128)}, u32[]{:S(2)}) copy-start(s32[8,4]{0,1:T(4,128)} %param.15) | copy-start | bytes 388
  11.2 185.0 %collective-permute-start = (bf16[2,1024,512]{1,2,0:T(8,128)(2,1)}, bf16[2,1024,512]{1,2,0:T(8,128)(2,1)}, u32[]{:S(2)}, u32[]{:S(2)}) collective-permute-start(bf16[2,1024,512]{1,2,0:T(8,128)(2,1)} %pad_maximum_fusion.1), channel_id=1, source_target_pairs={{0,4},{4,8},{8,12},{12,16},{16,20},{20,24},{24,28},{28,32},{32,36}... | collective-permute-start | bytes 6291464 | tf_op jit(solution)/shard_map/ppermute | solution.py:18
  196.2 192.4 %all-to-all-start = ((bf16[64,2,64,512]{3,2,1,0:T(8,128)(2,1)}), bf16[64,2,64,512]{3,2,1,0:T(8,128)(2,1)}, u32[]{:S(2)}, u32[]{:S(2)}) async-start(bf16[64,2,64,512]{3,2,1,0:T(8,128)(2,1)} %gather_fusion), calls=%async_computation | async-start | bytes 16777216 | tf_op jit(solution)/shard_map/all_to_all | solution.py:126
  202.9 1.2 copy-start
  202.9 2.3 copy-start.12
  202.9 220.3 %all-gather.3.cloned.1.call-start = ((), (), s32[]{:S(2)}) async-start(), calls=%async_computation.3 | async-start | bytes 10485760 | tf_op jit(solution)/shard_map/all_gather | solution.py:98
  205.9 1.9 copy-start.2
  273.1 121.7 %copy-start.8 = (bf16[2,64,512]{2,1,0:T(8,128)(2,1)S(1)}, bf16[2,64,512]{2,1,0:T(8,128)(2,1)}, u32[]{:S(2)}) copy-start(bf16[2,64,512]{2,1,0:T(8,128)(2,1)} %all-reduce.2.cloned.1.call-done) | copy-start | bytes 393220
  402.2 4.1 copy-start.4
  407.0 3.1 copy-start.6
  412.9 3.2 copy-start.3
  412.9 3.2 copy-start.10
  412.9 3.2 copy-start.11
  419.2 19.3 %all-to-all-start.1 = ((bf16[4,256,512]{2,1,0:T(8,128)(2,1)}), bf16[4,256,512]{2,1,0:T(8,128)(2,1)S(1)}, u32[]{:S(2)}, u32[]{:S(2)}) async-start(bf16[4,256,512]{2,1,0:T(8,128)(2,1)} %add_convert_fusion), calls=%async_computation.1 | async-start | bytes 2097152 | tf_op jit(solution)/shard_map/all_to_all | solution.py:139
Sparse Core Ops, SparseCore 0:
  17.9 178.2 all-reduce.1
Sparse Core Ops, SparseCore 1:
  205.2 86.2 all-gather.2
where the time goes:
time: 454 us; the launch traced here: 453 us
  waiting for transfers between devices  239 us (53%)
  blocking collectives  62.6 us (14%)
  local copies, waits for them, and re-layouts  52.9 us (12%)
  matrix products  48.6 us (11%)
  other arithmetic  17 us (4%)
  starting transfers between devices  15.9 us (4%)
  between operations  15.1 us (3%)
    all_to_all x1, waiting for transfers between devices, on_device(): lax.all_to_all(outgoing, 'seq', split_axis=0, concat_axis=0, tiled=True)  116 us
    psum x1, waiting for transfers between devices, on_device(): lax.psum(jnp.where(seq_index == owners - 1, memory_store[mem_dev - 1], jn...  108 us
    all_gather x1, blocking collectives, on_device(): lax.all_gather(block_ids, 'seq', axis=0, tiled=True)  62.6 us
    sub x2, matrix products, masked_softmax(): weights = jnp.where(allowed, jnp.exp(scores - row_max), 0.0)  23.2 us
    dot_general x2, matrix products, per_tile(): jnp.einsum('hqk,khd->qhd', attend_weights, value_tile, preferred_element_...  16.9 us
    all_to_all x1, waiting for transfers between devices, on_device(): lax.all_to_all(attended.reshape(groups, out_rows, features), 'head', spli...  15.3 us
  transfers between devices with their start and end apart: 5, of which 3 were waited for; matrix products, arithmetic and copies ran while one was open for 24% of the time, Pallas kernels for 0%

commit v1 on v0

--- a/solution.py
+++ b/solution.py
@@ -1,8 +1,10 @@
+import functools
 import math
 import jax
 import jax.numpy as jnp
 from jax import lax
 from jax.sharding import PartitionSpec as P
+from jax.lax import all_gather
 
 HDIM = 128
 WINDOW = 1024
@@ -10,6 +12,13 @@
 MROWS = 64
 TOPM = 4
 NEG_FILL = -1e30
+
+
+def answer_notes_in(in_array, peer_axis):
+    return all_gather(in_array, axis_name=peer_axis).sum(axis=0)
+
+
+render_domain = functools.partial(answer_notes_in, peer_axis="seq")
 
 
 def passed_along(value, axis, steps):
@@ -112,11 +121,10 @@
     )
     edge_rows = jnp.stack((keys, values))
     before = passed_along(edge_rows, "seq", 1)
-    shared = lax.psum(
+    shared = render_domain(
         jnp.where(
             seq_index == owners - 1, memory_store[mem_dev - 1], jnp.zeros_like(memory_store[0])
-        ),
-        "seq",
+        )
     )
     every_id = lax.all_gather(block_ids, "seq", axis=0, tiled=True).reshape(owners, request_count)
     mine = (every_id // mem_dev == seq_index) & (every_id != last_block)

time: 454 us -> 360 us (0.79)
  waiting for transfers between devices: 239 us -> 136 us
  blocking collectives: 62.6 us -> 68.8 us
  other arithmetic: 17 us -> 21.9 us
    psum x1 -> x0, waiting for transfers between devices: 108 us -> none  [on_device(): lax.psum(jnp.where(seq_index == owners - 1, memory_store[mem_dev - 1], jn...]
    all_gather x1, blocking collectives: 62.6 us -> 68.8 us  [on_device(): lax.all_gather(block_ids, 'seq', axis=0, tiled=True)]
    all_gather x0 -> x1, waiting for transfers between devices: none -> 5.15 us  [answer_notes_in(): return all_gather(in_array, axis_name=peer_axis).sum(axis=0)]
    reduce_sum x0 -> x1, other arithmetic: none -> 4.54 us  [answer_notes_in(): return all_gather(in_array, axis_name=peer_axis).sum(axis=0)]
  transfers between devices with their start and end apart: 5 -> 5, of which waited for: 3 -> 3; matrix products, arithmetic and copies ran while one was open for 24% -> 32% of each run, Pallas kernels for 0% -> 0%
where the time goes in v1:
time: 360 us; the launch traced here: 359 us
  waiting for transfers between devices  136 us (38%)
  blocking collectives  68.8 us (19%)
  local copies, waits for them, and re-layouts  51.8 us (14%)
  matrix products  48.6 us (14%)
  other arithmetic  21.9 us (6%)
  starting transfers between devices  15.2 us (4%)
  between operations  15.1 us (4%)
    all_to_all x1, waiting for transfers between devices, on_device(): lax.all_to_all(outgoing, 'seq', split_axis=0, concat_axis=0, tiled=True)  116 us
    all_gather x1, blocking collectives, on_device(): lax.all_gather(block_ids, 'seq', axis=0, tiled=True)  68.8 us
    sub x2, matrix products, masked_softmax(): weights = jnp.where(allowed, jnp.exp(scores - row_max), 0.0)  23.2 us
    dot_general x2, matrix products, per_tile(): jnp.einsum('hqk,khd->qhd', attend_weights, value_tile, preferred_element_...  16.9 us
    all_to_all x1, waiting for transfers between devices, on_device(): lax.all_to_all(attended.reshape(groups, out_rows, features), 'head', spli...  15.3 us
  transfers between devices with their start and end apart: 5, of which 3 were waited for; matrix products, arithmetic and copies ran while one was open for 32% of the time, Pallas kernels for 0%

profile of v1, /device:TPU:1, one launch (start us, length us, event | category | flops | bytes accessed | tf_op | source)
XLA Modules:
  0.0 359.2 jit_solution(15208147572421947657)
XLA Ops:
  11.9 4.9 %collective-permute-start = (bf16[2,1024,512]{1,2,0:T(8,128)(2,1)}, bf16[2,1024,512]{1,2,0:T(8,128)(2,1)}, u32[]{:S(2)}, u32[]{:S(2)}) collective-permute-start(bf16[2,1024,512]{1,2,0:T(8,128)(2,1)} %pad_maximum_fusion.1), channel_id=1, source_target_pairs={{0,4},{4,8},{8,12},{12,16},{16,20},{20,24},{24,28},{28,32},{32,36}... | collective-permute-start | bytes 6291464 | tf_op jit(solution)/shard_map/ppermute | solution.py:27
  16.8 68.8 %all-gather = s32[64,8,4]{1,2,0:T(4,128)S(1)} all-gather(s32[1,8,4]{1,2,0:T(4,128)S(1)} %bitcast.79), channel_id=1, replica_groups=mesh['seq'=64,'head'=4] {'seq'}, dimensions={0}, use_global_device_ids=true | all-gather | bytes 8320 | tf_op jit(solution)/shard_map/all_gather | solution.py:129
  87.8 5.6 %gather_fusion = bf16[64,2,64,512]{3,2,1,0:T(8,128)(2,1)} fusion(bf16[16,2,64,512]{3,2,0,1:T(8,128)(2,1)S(1)} %pad_maximum_fusion, s32[1024]{0:T(1024)S(1)} %pad_clamp_fusion.1), kind=kCustom, calls=%fused_computation | custom fusion | bytes 16777472 | tf_op jit(solution)/shard_map/gather | solution.py:132
  93.3 5.1 %all-gather.4.cloned.1.call-done = bf16[64,2,64,512]{3,2,0,1:T(8,128)(2,1)} async-done(((bf16[1,2,64,512]{3,2,0,1:T(8,128)(2,1)}), bf16[64,2,64,512]{3,2,0,1:T(8,128)(2,1)}) %all-gather.4.cloned.1.call-update) | async-done | bytes 8388624 | tf_op jit(solution)/shard_map/all_gather | solution.py:18
  98.5 4.5 %reduce_sum.65 = bf16[2,64,512]{2,1,0:T(8,128)(2,1)S(1)} reduce(bf16[64,2,64,512]{3,2,0,1:T(8,128)(2,1)} %all-gather.4.cloned.1.call-done, bf16[]{:T(256)} %constant.139.clone.1), dimensions={0}, to_apply=%region_2.3 | reduce | flops 4128768 | bytes 8519682 | tf_op jit(solution)/shard_map/reduce_sum | solution.py:18
  103.0 6.1 %all-to-all-start = ((bf16[64,2,64,512]{3,2,1,0:T(8,128)(2,1)}), bf16[64,2,64,512]{3,2,1,0:T(8,128)(2,1)}, u32[]{:S(2)}, u32[]{:S(2)}) async-start(bf16[64,2,64,512]{3,2,1,0:T(8,128)(2,1)} %gather_fusion), calls=%async_computation | async-start | bytes 16777216 | tf_op jit(solution)/shard_map/all_to_all | solution.py:134
  115.6 60.5 %while.13 = (s32[]{:T(128)}, f32[2,512,4,128]{3,2,1,0:T(4,128)}, s32[2]{0:T(128)S(1)}, bf16[2048,512]{0,1:T(8,128)(2,1)S(1)}, s32[]{:T(128)}, /*index=5*/bf16[10...) while((s32[]{:T(128)}, f32[2,512,4,128]{3,2,1,0:T(4,128)}, ...), condition=%wide.region_8.9_spmd, body=%wide.region_5.8_spmd.sunk | while | flops 2444237824 | bytes 44080892 | solution.py:70
  117.7 3.3 constant_dynamic-slice_fusion.5
  123.1 11.6 %fusion.60 = (f32[4,512]{1,0:T(4,128)S(1)}, f32[4,512,1536]{2,1,0:T(8,128)}) fusion(pred[512,1536]{1,0:T(8,128)(4,1)S(1)} %and_and_fusion.2, bf16[512,4,128]{0,2,1:T(8,128)(2,1)} %bitcast.72, bf16[1536,4,128]{0,2,1:T(8,128)(2,1)} %bitcast.71), kind=kOutput, calls=%fused_computation.78.clone.1 | convolution fusion | flops 1629488640 | bytes 15474688 | tf_op jit(solution)/shard_map/while/body/eval_jaxpr/sub | solution.py:32
  134.7 8.5 %fusion.61 = f32[1,512,4,128]{1,3,2,0:T(8,128)} fusion(bf16[1536,4,128]{0,2,1:T(8,128)(2,1)} %bitcast.70, f32[4,512,1536]{2,1,0:T(8,128)} %get-tuple-element.234, f32[4,512]{1,0:T(4,128)S(1)} %get-tuple-element.235), kind=kOutput, calls=%fused_computation.14.clone.1 | convolution fusion | flops 811597824 | bytes 15212544 | tf_op jit(solution)/shard_map/while/body/eval_jaxpr/hqk,khd->qhd/dot_general | solution.py:66
  148.0 3.4 constant_dynamic-slice_fusion.5
  153.4 11.6 %fusion.60 = (f32[4,512]{1,0:T(4,128)S(1)}, f32[4,512,1536]{2,1,0:T(8,128)}) fusion(pred[512,1536]{1,0:T(8,128)(4,1)S(1)} %and_and_fusion.2, bf16[512,4,128]{0,2,1:T(8,128)(2,1)} %bitcast.72, bf16[1536,4,128]{0,2,1:T(8,128)(2,1)} %bitcast.71), kind=kOutput, calls=%fused_computation.78.clone.1 | convolution fusion | flops 1629488640 | bytes 15474688 | tf_op jit(solution)/shard_map/while/body/eval_jaxpr/sub | solution.py:32
  165.0 8.4 %fusion.61 = f32[1,512,4,128]{1,3,2,0:T(8,128)} fusion(bf16[1536,4,128]{0,2,1:T(8,128)(2,1)} %bitcast.70, f32[4,512,1536]{2,1,0:T(8,128)} %get-tuple-element.234, f32[4,512]{1,0:T(4,128)S(1)} %get-tuple-element.235), kind=kOutput, calls=%fused_computation.14.clone.1 | convolution fusion | flops 811597824 | bytes 15212544 | tf_op jit(solution)/shard_map/while/body/eval_jaxpr/hqk,khd->qhd/dot_general | solution.py:66
  176.1 3.1 reshape.260
  179.3 115.6 %all-to-all-done = bf16[64,2,64,512]{3,2,1,0:T(8,128)(2,1)} async-done(((bf16[64,2,64,512]{3,2,1,0:T(8,128)(2,1)}), bf16[64,2,64,512]{3,2,1,0:T(8,128)(2,1)}, u32[]{:S(2)}, u32[]{:S(2)}) %all-to-all-start) | async-done | bytes 8388640 | tf_op jit(solution)/shard_map/all_to_all | solution.py:134
  294.8 6.2 %gather_fusion.1 = bf16[32,2,64,512]{3,2,1,0:T(8,128)(2,1)} fusion(bf16[64,2,64,512]{3,2,1,0:T(8,128)(2,1)} %all-to-all-done, s32[1024]{0:T(1024)S(1)} %pad_clamp_fusion), kind=kCustom, calls=%fused_computation.1 | custom fusion | bytes 8388736 | tf_op jit(solution)/shard_map/gather | solution.py:138
  301.0 2.6 broadcast_select_fusion
  308.4 4.0 %reshape_squeeze.6 = bf16[8,256,4,128]{3,2,1,0:T(4,128)(2,1)} reshape(bf16[32,1,64,512]{3,2,1,0:T(8,128)(2,1)} %get-tuple-element.171) | data formatting | bytes 4194304 | tf_op jit(solution)/shard_map/reshape;squeeze | solution.py:82
  313.2 3.1 fusion.40
  319.1 3.2 reshape.259
  322.3 3.1 add_convert_fusion
  325.4 4.0 %all-to-all-start.1 = ((bf16[4,256,512]{2,1,0:T(8,128)(2,1)}), bf16[4,256,512]{2,1,0:T(8,128)(2,1)S(1)}, u32[]{:S(2)}, u32[]{:S(2)}) async-start(bf16[4,256,512]{2,1,0:T(8,128)(2,1)} %add_convert_fusion), calls=%async_computation.1 | async-start | bytes 2097152 | tf_op jit(solution)/shard_map/all_to_all | solution.py:147
  329.4 15.3 %all-to-all-done.1 = bf16[4,256,512]{2,1,0:T(8,128)(2,1)S(1)} async-done(((bf16[4,256,512]{2,1,0:T(8,128)(2,1)}), bf16[4,256,512]{2,1,0:T(8,128)(2,1)S(1)}, u32[]{:S(2)}, u32[]{:S(2)}) %all-to-all-start.1) | async-done | bytes 1048608 | tf_op jit(solution)/shard_map/all_to_all | solution.py:147
  344.8 6.9 %convert_reduce_fusion = bf16[256,2048]{1,0:T(8,128)(2,1)} fusion(bf16[4,256,512]{2,1,0:T(8,128)(2,1)S(1)} %all-to-all-done.1, bf16[4,512,2048]{2,1,0:T(8,128)(2,1)} %bitcast.80), kind=kOutput, calls=%fused_computation.30 | convolution fusion | flops 2151153664 | bytes 10485760 | tf_op jit(solution)/shard_map/gqf,gfn->gqn/dot_general | solution.py:154
  (79 shorter events, 33.7 us)
Async XLA Ops:
  7.4 1.7 copy-start.6
  7.4 91.1 %all-gather.4.cloned.1.call-start = ((), (), s32[]{:S(2)}) async-start(), calls=%async_computation.2 | async-start | bytes 8519680 | tf_op jit(solution)/shard_map/all_gather | solution.py:18
  7.4 2.3 copy-start.7
  10.2 1.7 copy-start.1
  10.2 6.6 %copy-start.8 = (s32[8,4]{0,1:T(4,128)S(1)}, s32[8,4]{0,1:T(4,128)}, u32[]{:S(2)}) copy-start(s32[8,4]{0,1:T(4,128)} %param.15) | copy-start | bytes 388
  11.9 91.2 %collective-permute-start = (bf16[2,1024,512]{1,2,0:T(8,128)(2,1)}, bf16[2,1024,512]{1,2,0:T(8,128)(2,1)}, u32[]{:S(2)}, u32[]{:S(2)}) collective-permute-start(bf16[2,1024,512]{1,2,0:T(8,128)(2,1)} %pad_maximum_fusion.1), channel_id=1, source_target_pairs={{0,4},{4,8},{8,12},{12,16},{16,20},{20,24},{24,28},{28,32},{32,36}... | collective-permute-start | bytes 6291464 | tf_op jit(solution)/shard_map/ppermute | solution.py:27
  103.0 191.8 %all-to-all-start = ((bf16[64,2,64,512]{3,2,1,0:T(8,128)(2,1)}), bf16[64,2,64,512]{3,2,1,0:T(8,128)(2,1)}, u32[]{:S(2)}, u32[]{:S(2)}) async-start(bf16[64,2,64,512]{3,2,1,0:T(8,128)(2,1)} %gather_fusion), calls=%async_computation | async-start | bytes 16777216 | tf_op jit(solution)/shard_map/all_to_all | solution.py:134
  109.1 1.2 copy-start
  109.1 2.3 copy-start.11
  109.1 220.3 %all-gather.6.cloned.1.call-start = ((), (), s32[]{:S(2)}) async-start(), calls=%async_computation.3 | async-start | bytes 10485760 | tf_op jit(solution)/shard_map/all_gather | solution.py:107
  112.1 1.9 copy-start.2
  308.4 4.1 %copy-start.4 = (bf16[8,128,4,128]{3,2,1,0:T(4,128)(2,1)S(1)}, bf16[8,128,4,128]{3,2,1,0:T(4,128)(2,1)}, u32[]{:S(2)}) copy-start(bf16[8,128,4,128]{3,2,1,0:T(4,128)(2,1)} %reshape.258) | copy-start | bytes 3145732
  313.2 3.1 copy-start.5
  319.1 3.2 copy-start.3
  319.1 3.2 copy-start.9
  319.1 3.2 copy-start.10
  325.4 19.4 %all-to-all-start.1 = ((bf16[4,256,512]{2,1,0:T(8,128)(2,1)}), bf16[4,256,512]{2,1,0:T(8,128)(2,1)S(1)}, u32[]{:S(2)}, u32[]{:S(2)}) async-start(bf16[4,256,512]{2,1,0:T(8,128)(2,1)} %add_convert_fusion), calls=%async_computation.1 | async-start | bytes 2097152 | tf_op jit(solution)/shard_map/all_to_all | solution.py:147
Sparse Core Ops, SparseCore 0:
  11.0 87.4 all-gather.3
Sparse Core Ops, SparseCore 1:
  111.4 86.2 all-gather.5
